TPU v7x, 256 devices: a whole 4x4x8 slice. The times are simulated.
256 devices in a mesh: heads: 32 (over z_hi, y, x), width: 8 (over z_lo, core).
Axes of the slice: x: 4, y: 4, z: 8 (z_hi: 2, z_lo: 4; z = z_hi * 4 + z_lo), core: 2. Of those that a mesh axis runs over, the one named last changes fastest.
Arguments:
- states: bfloat16 [1536, 6144], P('heads', 'width'), may hold values from -6 to 6
- segment_ids: int32 [1536], replicated, may hold values from 0 to 11, never falling along the last dimension, each value on 1 to 1344 neighbouring positions
- attn_gain: float32 [6144], P('width'), may hold values from 0.1 to 1.9
- attn_shift: float32 [6144], P('width'), may hold values from -3 to 3
- mlp_gain: float32 [6144], P('width'), may hold values from 0.1 to 1.9
- mlp_shift: float32 [6144], P('width'), may hold values from -3 to 3
- qkv_weight: bfloat16 [6144, 18432], P('width', 'heads'), may hold values from -0.078125 to 0.078125
- qkv_bias: float32 [18432], P('heads'), may hold values from -6 to 6
- dense_weight: bfloat16 [6144, 6144], P('heads', 'width'), may hold values from -0.078125 to 0.078125
- dense_bias: float32 [6144], P('width'), may hold values from -2 to 2
- up_weight: bfloat16 [6144, 24576], P('width', 'heads'), may hold values from -0.078125 to 0.078125
- up_bias: float32 [24576], P('heads'), may hold values from -3 to 3
- down_weight: bfloat16 [24576, 6144], P('heads', 'width'), may hold values from -0.0390625 to 0.0390625
- down_bias: float32 [6144], P('width'), may hold values from -2 to 2
Outputs:
- layer_out: bfloat16 [1536, 6144], P('heads', 'width')
- key_cache: bfloat16 [1536, 6144], P('width', 'heads')
- value_cache: bfloat16 [1536, 6144], P('width', 'heads')
Inputs may be any that keep to these rules, and one draw needn't show every extreme that they name: `segment_ids`: document numbers never fall along the tokens; each document has 1 to 1344 tokens and one has exactly 1344.
All inputs are finite; a program needn't handle non-finite values.
Results may differ from a plain program's by a relative error of at most 0.017.
Values may be sent and summed in bfloat16 or wider, within the bound.
No kernel may reach another device: no remote copies, remote signals or barrier semaphores. Data moves between devices by JAX's collectives and lax.ppermute only.
A program may use at most 64 MiB of HBM per device.

v0:
```python
import jax
import jax.numpy as jnp
from jax import lax
from jax.sharding import PartitionSpec as P

HD = 96
ROT = 24
D = 6144
norm_epsilon = 1e-05


def positions_of(segments):
    count = segments.shape[0]
    row_index = jnp.arange(count, dtype=jnp.int32)
    change = jnp.concatenate([jnp.ones((1,), bool), segments[1:] != segments[:-1]])
    first = lax.cummax(jnp.where(change, row_index, 0), axis=0)
    return (row_index - first).astype(jnp.float32)


def rotary(values, positions):
    half_rot = ROT // 2
    inverse = 10000.0 ** (-(jnp.arange(half_rot, dtype=jnp.float32) * 2.0 / ROT))
    angles = positions[:, None] * inverse[None, :]
    cosine = jnp.cos(angles)[:, None, :]
    sine_part = jnp.sin(angles)[:, None, :]
    first_half = values[..., :half_rot]
    second_half = values[..., half_rot:ROT]
    return jnp.concatenate(
        [
            first_half * cosine - second_half * sine_part,
            second_half * cosine + first_half * sine_part,
            values[..., ROT:],
        ],
        axis=-1,
    )


HEADS = ("hz", "hy", "hx")
WIDTH = ("wz", "wc")


def gather_heads(block):
    rows, cols = block.shape
    ny, nx = (lax.axis_size("hy"), lax.axis_size("hx"))
    spread = jnp.broadcast_to(block[None], (ny * nx,) + block.shape)
    block = lax.all_to_all(spread, ("hy", "hx"), 0, 0, tiled=False)
    nz = lax.axis_size("hz")
    block = block.reshape(ny, nx, nz, rows // nz, cols).transpose(2, 0, 1, 3, 4)
    return block.reshape(-1, cols)


def reduce_heads(partial):
    nz, ny, nx = [lax.axis_size(a) for a in HEADS]
    cols = partial.shape[1]
    rows = partial.shape[0] // (nz * ny * nx)
    part = partial.reshape(nz, ny * nx, rows, cols).transpose(1, 0, 2, 3)
    part = lax.all_to_all(part, ("hy", "hx"), 0, 0, tiled=False)
    total = jnp.sum(part.astype(jnp.float32), 0)
    part = lax.all_to_all(total.astype(jnp.bfloat16), "hz", 0, 0, tiled=False)
    return jnp.sum(part.astype(jnp.float32), 0)


def on_device(
    states,
    segment_ids,
    attn_gain,
    attn_shift,
    mlp_gain,
    mlp_shift,
    qkv_weight,
    qkv_bias,
    dense_weight,
    dense_bias,
    up_weight,
    up_bias,
    down_weight,
    down_bias,
):
    floats = states.astype(jnp.float32)
    nz = lax.axis_size("hz")
    z = lax.axis_index("hz")
    swaps = [
        lax.ppermute(states, "hz", [(i, (i + k) % nz) for i in range(nz)]) for k in range(1, nz)
    ]
    local = jnp.stack([jnp.sum(floats, -1), jnp.sum(floats * floats, -1)])
    group = nz * lax.axis_size(WIDTH)
    every = lax.all_to_all(
        jnp.broadcast_to(local[None], (group,) + local.shape), ("hz",) + WIDTH, 0, 0, tiled=False
    )
    stats = jnp.sum(every.reshape(nz, -1, 2, local.shape[1]), 1)
    pair = jnp.stack([states] + swaps)
    by_z = jnp.take(pair, (z - jnp.arange(nz)) % nz, axis=0).astype(jnp.float32)
    row_mean = (stats[:, 0] / D)[..., None]
    row_var = (stats[:, 1] / D)[..., None] - row_mean * row_mean
    normed = ((by_z - row_mean) * lax.rsqrt(row_var + norm_epsilon)).astype(jnp.bfloat16)
    qkv_cols = qkv_weight.shape[1]
    heads_dev = qkv_cols // (3 * HD)
    block_f = gather_heads(normed.reshape(-1, normed.shape[2])).astype(jnp.float32)
    attn_in = (block_f * attn_gain + attn_shift).astype(jnp.bfloat16)
    mlp_in = (block_f * mlp_gain + mlp_shift).astype(jnp.bfloat16)
    projected = jnp.concatenate(
        [
            jnp.dot(attn_in, qkv_weight, preferred_element_type=jnp.float32),
            jnp.dot(mlp_in, up_weight, preferred_element_type=jnp.float32),
        ],
        axis=1,
    )
    summed_proj = lax.psum(projected.astype(jnp.bfloat16), WIDTH)
    all_tokens = projected.shape[0]
    own_rows = all_tokens // lax.axis_size(WIDTH)
    row_zero = lax.axis_index(WIDTH) * own_rows
    positions = positions_of(segment_ids)
    own_segments = lax.dynamic_slice_in_dim(segment_ids, row_zero, own_rows)
    own_index = row_zero + jnp.arange(own_rows, dtype=jnp.int32)
    score_scale = 1.0 / HD**0.5
    own_positions = lax.dynamic_slice_in_dim(positions, row_zero, own_rows)
    shaped = (summed_proj[:, :qkv_cols].astype(jnp.float32) + qkv_bias).reshape(
        all_tokens, heads_dev, 3, HD
    )
    own_shaped = lax.dynamic_slice_in_dim(shaped, row_zero, own_rows)
    queries = rotary(own_shaped[:, :, 0, :], own_positions).astype(jnp.bfloat16)
    key_heads = rotary(shaped[:, :, 1, :], positions).astype(jnp.bfloat16)
    value_heads = shaped[:, :, 2, :].astype(jnp.bfloat16)
    width_cols = heads_dev * HD
    key_cache = lax.dynamic_slice_in_dim(key_heads, row_zero, own_rows).reshape(-1, width_cols)
    value_cache = lax.dynamic_slice_in_dim(value_heads, row_zero, own_rows).reshape(-1, width_cols)
    run_max = jnp.full((heads_dev, own_rows), -1e30, jnp.float32)
    count = all_tokens
    scores = (
        jnp.einsum("rhd,nhd->hrn", queries, key_heads, preferred_element_type=jnp.float32)
        * score_scale
    )
    key_index = jnp.arange(count, dtype=jnp.int32)
    allowed = (own_segments[:, None] == segment_ids[None, :]) & (
        key_index[None, :] <= own_index[:, None]
    )
    scores = jnp.where(allowed[None], scores, -1e30)
    new_max = jnp.maximum(run_max, jnp.max(scores, -1))
    weights = jnp.where(allowed[None], jnp.exp(scores - new_max[..., None]), 0.0)
    new_sum = jnp.sum(weights, -1)
    mixed = jnp.einsum(
        "hrn,nhd->hrd",
        weights.astype(jnp.bfloat16),
        value_heads,
        preferred_element_type=jnp.float32,
    )
    attended = (
        (mixed / new_sum[..., None])
        .transpose(1, 0, 2)
        .reshape(own_rows, heads_dev * HD)
        .astype(jnp.bfloat16)
    )
    attn_part = jnp.dot(
        lax.all_to_all(
            jnp.broadcast_to(attended[None], (lax.axis_size(WIDTH),) + attended.shape),
            WIDTH,
            0,
            0,
            tiled=False,
        ).reshape(-1, attended.shape[1]),
        dense_weight,
        preferred_element_type=jnp.float32,
    )
    hidden = jax.nn.gelu(
        summed_proj[:, qkv_cols:].astype(jnp.float32) + up_bias, approximate=False
    ).astype(jnp.bfloat16)
    hidden = lax.optimization_barrier(hidden)
    mlp_part = jnp.dot(hidden, down_weight, preferred_element_type=jnp.float32)
    summed = reduce_heads((attn_part + mlp_part).astype(jnp.bfloat16))
    layer_out = (floats + summed + dense_bias + down_bias).astype(jnp.bfloat16)
    return (layer_out, key_cache, value_cache)


def solution(mesh):
    devices = mesh.devices.reshape(2, 4, 4, 4, 2)
    fine = jax.sharding.Mesh(devices, HEADS + WIDTH)
    in_specs = (
        P(HEADS, WIDTH),
        P(),
        P(WIDTH),
        P(WIDTH),
        P(WIDTH),
        P(WIDTH),
        P(WIDTH, HEADS),
        P(HEADS),
        P(HEADS, WIDTH),
        P(WIDTH),
        P(WIDTH, HEADS),
        P(HEADS),
        P(HEADS, WIDTH),
        P(WIDTH),
    )
    out_specs = (P(HEADS, WIDTH), P(WIDTH, HEADS), P(WIDTH, HEADS))
    return jax.shard_map(
        on_device, mesh=fine, in_specs=in_specs, out_specs=out_specs, check_vma=False
    )
```

profile of v0, /device:TPU:2, one launch (start us, length us, event | category | flops | bytes accessed | tf_op | source)
XLA Modules:
  0.0 273.8 jit_solution(16590568960911276245)
XLA Ops:
  7.2 7.3 %collective-permute-start = (bf16[48,768]{1,0:T(8,128)(2,1)}, bf16[48,768]{1,0:T(8,128)(2,1)S(1)}, u32[]{:S(2)}, u32[]{:S(2)}) collective-permute-start(bf16[48,768]{1,0:T(8,128)(2,1)} %param.14), channel_id=1, source_target_pairs={{0,128},{128,0},{1,129},{129,1},{2,130},{130,2},{3,131},{131,3},{4... | collective-permute-start | bytes 221192 | tf_op jit(solution)/shard_map/ppermute | solution.py:83
  14.5 1.0 convert_reduce_fusion.1
  16.1 3.5 %all-to-all-start = ((f32[16,2,48]{2,1,0:T(2,128)}), f32[16,2,48]{2,1,0:T(2,128)S(1)}, u32[]{:S(2)}, u32[]{:S(2)}) async-start(f32[16,2,48]{2,1,0:T(2,128)} %broadcast_in_dim.49), calls=%async_computation | async-start | bytes 32768 | tf_op jit(solution)/shard_map/all_to_all | solution.py:87
  19.9 7.3 %all-to-all-done = f32[16,2,48]{2,1,0:T(2,128)S(1)} async-done(((f32[16,2,48]{2,1,0:T(2,128)}), f32[16,2,48]{2,1,0:T(2,128)S(1)}, u32[]{:S(2)}, u32[]{:S(2)}) %all-to-all-start) | async-done | bytes 6176 | tf_op jit(solution)/shard_map/all_to_all | solution.py:87
  27.4 0.9 pad_maximum_fusion.2
  29.2 37.4 %all_to_all.25 = bf16[16,96,768]{2,1,0:T(8,128)(2,1)S(1)} all-to-all(bf16[16,96,768]{2,1,0:T(8,128)(2,1)S(1)} %broadcast_in_dim.50), channel_id=1, replica_groups=mesh['hz'=2,'hy'=4,'hx'=4,'wz'=4,'wc'=2] {'hy','hx'}, dimensions={0} | all-to-all | bytes 4718592 | tf_op jit(solution)/shard_map/all_to_all | solution.py:46
  67.9 1.1 fusion.4
  69.1 1.6 convolution_convert_fusion.1
  70.7 2.1 convolution_convert_fusion
  72.8 2.2 pad_maximum_fusion
  77.3 99.5 %all-reduce.2.cloned.1.call-done = bf16[1536,1344]{0,1:T(8,128)(2,1)} async-done(((bf16[1536,1344]{0,1:T(8,128)(2,1)}), bf16[1536,1344]{0,1:T(8,128)(2,1)}) %all-reduce.2.cloned.1.call-update) | async-done | bytes 4128784 | tf_op jit(solution)/shard_map/psum | solution.py:108
  176.8 1.8 convert_add_fusion.1
  178.7 1.6 copy-done.1
  180.9 0.9 copy-done.2
  181.8 0.8 fusion.53
  182.6 0.7 fusion.18
  183.4 2.0 fusion.32
  185.4 1.0 broadcast_in_dim.93
  186.4 3.7 %all-to-all-start.2 = ((bf16[8,192,192]{2,1,0:T(8,128)(2,1)}), bf16[8,192,192]{2,1,0:T(8,128)(2,1)S(1)}, u32[]{:S(2)}, u32[]{:S(2)}) async-start(bf16[8,192,192]{2,1,0:T(8,128)(2,1)} %broadcast_in_dim.93), calls=%async_computation.2 | async-start | bytes 1572864 | tf_op jit(solution)/shard_map/all_to_all | solution.py:154
  190.2 12.2 %fusion.2 = bf16[1536,768]{0,1:T(8,128)(2,1)S(1)} fusion(bf16[1536,1344]{0,1:T(8,128)(2,1)} %all-reduce.2.cloned.1.call-done, f32[768]{0:T(1024)S(1)} %copy-done.12), kind=kLoop, calls=%fused_computation.4 | loop fusion | flops 79036416 | bytes 4721664 | tf_op jit(solution)/shard_map/convert_element_type | solution.py:166
  202.4 4.2 %fusion.55 = f32[1536,768]{1,0:T(8,128)} fusion(bf16[1536,768]{0,1:T(8,128)(2,1)S(1)} %fusion.2, bf16[768,768]{1,0:T(8,128)(2,1)S(1)} %copy-done.13), kind=kOutput, calls=%fused_computation.116 | convolution fusion | flops 1811939328 | bytes 8257536 | tf_op jit(solution)/shard_map/dot_general | solution.py:168
  206.6 4.3 %all-to-all-done.2 = bf16[8,192,192]{2,1,0:T(8,128)(2,1)S(1)} async-done(((bf16[8,192,192]{2,1,0:T(8,128)(2,1)}), bf16[8,192,192]{2,1,0:T(8,128)(2,1)S(1)}, u32[]{:S(2)}, u32[]{:S(2)}) %all-to-all-start.2) | async-done | bytes 589856 | tf_op jit(solution)/shard_map/all_to_all | solution.py:154
  210.9 3.1 %add_convert_fusion = bf16[1536,768]{1,0:T(8,128)(2,1)S(1)} fusion(f32[1536,768]{1,0:T(8,128)} %fusion.55, bf16[1536,192]{1,0:T(8,128)(2,1)S(1)} %bitcast.73, bf16[192,768]{1,0:T(8,128)(2,1)S(1)} %copy-done.3), kind=kOutput, calls=%fused_computation.12 | convolution fusion | flops 455344128 | bytes 7962624 | tf_op jit(solution)/shard_map/dot_general | solution.py:153
  214.2 36.6 %all_to_all.26 = bf16[16,2,48,768]{3,2,1,0:T(8,128)(2,1)S(1)} all-to-all(bf16[16,2,48,768]{3,2,1,0:T(8,128)(2,1)S(1)} %bitcast.67), channel_id=1, replica_groups=mesh['hz'=2,'hy'=4,'hx'=4,'wz'=4,'wc'=2] {'hy','hx'}, dimensions={0} | all-to-all | bytes 4718592 | tf_op jit(solution)/shard_map/all_to_all | solution.py:57
  250.9 1.0 reduce_sum.61
  251.9 5.0 %all-to-all-start.4 = ((bf16[2,48,768]{2,1,0:T(8,128)(2,1)}), bf16[2,48,768]{2,1,0:T(8,128)(2,1)S(1)}, u32[]{:S(2)}, u32[]{:S(2)}) async-start(bf16[2,48,768]{2,1,0:T(8,128)(2,1)} %reduce_sum.61), calls=%async_computation.4 | async-start | bytes 294912 | tf_op jit(solution)/shard_map/all_to_all | solution.py:59
  256.9 1.1 constant_dynamic-slice_fusion
  258.0 0.7 copy.80
  258.7 1.0 constant_dynamic-slice_fusion.1
  259.7 0.7 copy.79
  260.5 4.9 %all-to-all-done.4 = bf16[2,48,768]{2,1,0:T(8,128)(2,1)S(1)} async-done(((bf16[2,48,768]{2,1,0:T(8,128)(2,1)}), bf16[2,48,768]{2,1,0:T(8,128)(2,1)S(1)}, u32[]{:S(2)}, u32[]{:S(2)}) %all-to-all-start.4) | async-done | bytes 147488 | tf_op jit(solution)/shard_map/all_to_all | solution.py:59
  265.4 1.5 fusion.39
  (76 shorter events, 6.7 us)
Async XLA Ops:
  7.2 63.5 %copy-start = (bf16[768,768]{1,0:T(8,128)(2,1)S(1)}, bf16[768,768]{1,0:T(8,128)(2,1)}, u32[]{:S(2)}) copy-start(bf16[768,768]{1,0:T(8,128)(2,1)} %param.24) | copy-start | bytes 3538948
  7.2 20.2 %collective-permute-start = (bf16[48,768]{1,0:T(8,128)(2,1)}, bf16[48,768]{1,0:T(8,128)(2,1)S(1)}, u32[]{:S(2)}, u32[]{:S(2)}) collective-permute-start(bf16[48,768]{1,0:T(8,128)(2,1)} %param.14), channel_id=1, source_target_pairs={{0,128},{128,0},{1,129},{129,1},{2,130},{130,2},{3,131},{131,3},{4... | collective-permute-start | bytes 221192 | tf_op jit(solution)/shard_map/ppermute | solution.py:83
  16.1 11.1 %all-to-all-start = ((f32[16,2,48]{2,1,0:T(2,128)}), f32[16,2,48]{2,1,0:T(2,128)S(1)}, u32[]{:S(2)}, u32[]{:S(2)}) async-start(f32[16,2,48]{2,1,0:T(2,128)} %broadcast_in_dim.49), calls=%async_computation | async-start | bytes 32768 | tf_op jit(solution)/shard_map/all_to_all | solution.py:87
  19.6 157.1 %all-reduce.2.cloned.1.call-start = ((), (), s32[]{:S(2)}) async-start(), calls=%async_computation.5 | async-start | bytes 8257536 | tf_op jit(solution)/shard_map/psum | solution.py:108
  67.2 0.7 copy-start.5
  67.2 0.7 copy-start.6
  67.2 0.7 copy-start.7
  67.2 0.7 copy-start.8
  67.9 1.2 copy-start.14
  72.8 2.3 copy-start.4
  72.8 103.9 %copy-start.9 = (f32[576]{0:T(1024)S(1)}, f32[576]{0:T(1024)}, u32[]{:S(2)}) copy-start(f32[576]{0:T(1024)} %param.21) | copy-start | bytes 6916
  178.5 1.8 copy-start.1
  180.9 0.9 copy-start.2
  182.6 7.6 %copy-start.12 = (f32[768]{0:T(1024)S(1)}, f32[768]{0:T(1024)}, u32[]{:S(2)}) copy-start(f32[768]{0:T(1024)} %param.25) | copy-start | bytes 9220
  185.3 17.0 %copy-start.13 = (bf16[768,768]{1,0:T(8,128)(2,1)S(1)}, bf16[768,768]{1,0:T(8,128)(2,1)}, u32[]{:S(2)}) copy-start(bf16[768,768]{1,0:T(8,128)(2,1)} %param.26) | copy-start | bytes 3538948
  186.4 24.4 %all-to-all-start.2 = ((bf16[8,192,192]{2,1,0:T(8,128)(2,1)}), bf16[8,192,192]{2,1,0:T(8,128)(2,1)S(1)}, u32[]{:S(2)}, u32[]{:S(2)}) async-start(bf16[8,192,192]{2,1,0:T(8,128)(2,1)} %broadcast_in_dim.93), calls=%async_computation.2 | async-start | bytes 1572864 | tf_op jit(solution)/shard_map/all_to_all | solution.py:154
  202.3 8.5 %copy-start.3 = (bf16[192,768]{1,0:T(8,128)(2,1)S(1)}, bf16[192,768]{1,0:T(8,128)(2,1)}, u32[]{:S(2)}) copy-start(bf16[192,768]{1,0:T(8,128)(2,1)} %param.22) | copy-start | bytes 884740
  214.2 51.2 %copy-start.10 = (f32[768]{0:T(1024)S(1)}, f32[768]{0:T(1024)}, u32[]{:S(2)}) copy-start(f32[768]{0:T(1024)} %param.27) | copy-start | bytes 9220
  214.2 51.2 %copy-start.11 = (f32[768]{0:T(1024)S(1)}, f32[768]{0:T(1024)}, u32[]{:S(2)}) copy-start(f32[768]{0:T(1024)} %param.23) | copy-start | bytes 9220
  251.9 13.5 %all-to-all-start.4 = ((bf16[2,48,768]{2,1,0:T(8,128)(2,1)}), bf16[2,48,768]{2,1,0:T(8,128)(2,1)S(1)}, u32[]{:S(2)}, u32[]{:S(2)}) async-start(bf16[2,48,768]{2,1,0:T(8,128)(2,1)} %reduce_sum.61), calls=%async_computation.4 | async-start | bytes 294912 | tf_op jit(solution)/shard_map/all_to_all | solution.py:59
Sparse Core Ops, SparseCore 0:
  75.2 101.5 all-reduce.1
where the time goes:
time: 275 us; the launch traced here: 274 us
  waiting for transfers between devices  116 us (42%)
  blocking collectives  74 us (27%)
  other arithmetic  25.1 us (9%)
  starting transfers between devices  19.6 us (7%)
  between operations  14.4 us (5%)
  matrix products  13.7 us (5%)
  local copies, waits for them, and re-layouts  11 us (4%)
    psum x1, waiting for transfers between devices, on_device(): summed_proj = lax.psum(projected.astype(jnp.bfloat16), WIDTH)  99.5 us
    all_to_all x1, blocking collectives, gather_heads(): block = lax.all_to_all(spread, ('hy', 'hx'), 0, 0, tiled=False)  37.4 us
    all_to_all x1, blocking collectives, reduce_heads(): part = lax.all_to_all(part, ('hy', 'hx'), 0, 0, tiled=False)  36.6 us
    convert_element_type x1, other arithmetic, on_device(): hidden = jax.nn.gelu(summed_proj[:, qkv_cols:].astype(jnp.float32) + up_b...  12.2 us
    all_to_all x1, waiting for transfers between devices, on_device(): lax.all_to_all(jnp.broadcast_to(local[None], (group,) + local.shape), ('h...  7.28 us
    ppermute x1, starting transfers between devices, on_device(): lax.ppermute(states, 'hz', [(i, (i + k) % nz) for i in range(nz)])  7.28 us
  transfers between devices with their start and end apart: 5, of which 4 were waited for; matrix products, arithmetic and copies ran while one was open for 9% of the time, Pallas kernels for 0%

commit v1 on v0

--- a/solution.py
+++ b/solution.py
@@ -105,7 +105,7 @@
         ],
         axis=1,
     )
-    summed_proj = lax.psum(projected.astype(jnp.bfloat16), WIDTH)
+    summed_proj = jnp.sum(lax.all_gather(projected.astype(jnp.bfloat16), WIDTH), axis=0)
     all_tokens = projected.shape[0]
     own_rows = all_tokens // lax.axis_size(WIDTH)
     row_zero = lax.axis_index(WIDTH) * own_rows

time: 275 us -> 510 us (1.85)
  waiting for transfers between devices: 116 us -> 361 us
  blocking collectives: 74 us -> 37.4 us
  other arithmetic: 25.1 us -> 39.1 us
  starting transfers between devices: 19.6 us -> 26.9 us
    all_gather x0 -> x1, waiting for transfers between devices: none -> 316 us  [on_device(): lax.all_gather(projected.astype(jnp.bfloat16), WIDTH)]
    psum x1 -> x0, waiting for transfers between devices: 99.5 us -> none  [on_device(): summed_proj = lax.psum(projected.astype(jnp.bfloat16), WIDTH)]
    all_to_all x1 -> x0, blocking collectives: 36.6 us -> none  [reduce_heads(): part = lax.all_to_all(part, ('hy', 'hx'), 0, 0, tiled=False)]
    all_to_all x0 -> x1, waiting for transfers between devices: none -> 26.4 us  [reduce_heads(): part = lax.all_to_all(part, ('hy', 'hx'), 0, 0, tiled=False)]
    reduce_sum x0 -> x1, other arithmetic: none -> 14.1 us  [on_device(): jnp.sum(lax.all_gather(projected.astype(jnp.bfloat16), WIDTH), axis=0)]
    all_to_all x0 -> x1, starting transfers between devices: none -> 7.41 us  [reduce_heads(): part = lax.all_to_all(part, ('hy', 'hx'), 0, 0, tiled=False)]
  transfers between devices with their start and end apart: 5 -> 6, of which waited for: 4 -> 5; matrix products, arithmetic and copies ran while one was open for 9% -> 5% of each run, Pallas kernels for 0% -> 0%
where the time goes in v1:
time: 510 us; the launch traced here: 505 us
  waiting for transfers between devices  361 us (71%)
  other arithmetic  39.1 us (8%)
  blocking collectives  37.4 us (7%)
  starting transfers between devices  26.9 us (5%)
  between operations  14.5 us (3%)
  matrix products  13.7 us (3%)
  local copies, waits for them, and re-layouts  13 us (3%)
    all_gather x1, waiting for transfers between devices, on_device(): lax.all_gather(projected.astype(jnp.bfloat16), WIDTH)  316 us
    all_to_all x1, blocking collectives, gather_heads(): block = lax.all_to_all(spread, ('hy', 'hx'), 0, 0, tiled=False)  37.4 us
    all_to_all x1, waiting for transfers between devices, reduce_heads(): part = lax.all_to_all(part, ('hy', 'hx'), 0, 0, tiled=False)  26.4 us
    reduce_sum x1, other arithmetic, on_device(): jnp.sum(lax.all_gather(projected.astype(jnp.bfloat16), WIDTH), axis=0)  14.1 us
    convert_element_type x1, other arithmetic, on_device(): hidden = jax.nn.gelu(summed_proj[:, qkv_cols:].astype(jnp.float32) + up_b...  12.2 us
  transfers between devices with their start and end apart: 6, of which 5 were waited for; matrix products, arithmetic and copies ran while one was open for 5% of the time, Pallas kernels for 0%

profile of v1, /device:TPU:2, one launch (start us, length us, event | category | flops | bytes accessed | tf_op | source)
XLA Modules:
  0.0 505.4 jit_solution(3123485457076879958)
XLA Ops:
  7.2 7.3 %collective-permute-start = (bf16[48,768]{1,0:T(8,128)(2,1)}, bf16[48,768]{1,0:T(8,128)(2,1)S(1)}, u32[]{:S(2)}, u32[]{:S(2)}) collective-permute-start(bf16[48,768]{1,0:T(8,128)(2,1)} %param.14), channel_id=1, source_target_pairs={{0,128},{128,0},{1,129},{129,1},{2,130},{130,2},{3,131},{131,3},{4... | collective-permute-start | bytes 221192 | tf_op jit(solution)/shard_map/ppermute | solution.py:83
  14.5 1.0 convert_reduce_fusion.1
  16.1 3.5 all-to-all-start
  19.9 7.3 %all-to-all-done = f32[16,2,48]{2,1,0:T(2,128)S(1)} async-done(((f32[16,2,48]{2,1,0:T(2,128)}), f32[16,2,48]{2,1,0:T(2,128)S(1)}, u32[]{:S(2)}, u32[]{:S(2)}) %all-to-all-start) | async-done | bytes 6176 | tf_op jit(solution)/shard_map/all_to_all | solution.py:87
  27.4 0.9 pad_maximum_fusion.2
  29.2 37.4 %all_to_all.25 = bf16[16,96,768]{2,1,0:T(8,128)(2,1)S(1)} all-to-all(bf16[16,96,768]{2,1,0:T(8,128)(2,1)S(1)} %broadcast_in_dim.50), channel_id=1, replica_groups=mesh['hz'=2,'hy'=4,'hx'=4,'wz'=4,'wc'=2] {'hy','hx'}, dimensions={0} | all-to-all | bytes 4718592 | tf_op jit(solution)/shard_map/all_to_all | solution.py:46
  67.9 1.1 fusion.4
  69.0 2.1 fusion.18
  71.1 1.6 fusion.19
  72.7 2.2 pad_maximum_fusion
  77.2 316.2 %all-gather.2.cloned.1.call-done = bf16[8,1536,1344]{1,2,0:T(8,128)(2,1)} async-done(((bf16[1,1536,1344]{1,2,0:T(8,128)(2,1)}), bf16[8,1536,1344]{1,2,0:T(8,128)(2,1)}) %all-gather.2.cloned.1.call-update) | async-done | bytes 33030160 | tf_op jit(solution)/shard_map/all_gather | solution.py:108
  393.4 14.1 %reduce_sum.72 = bf16[1536,1344]{0,1:T(8,128)(2,1)} reduce(bf16[8,1536,1344]{1,2,0:T(8,128)(2,1)} %all-gather.2.cloned.1.call-done, bf16[]{:T(256)} %constant.34.clone.1), dimensions={0}, to_apply=%region_3.4 | reduce | flops 14450688 | bytes 37158912 | tf_op jit(solution)/shard_map/reduce_sum | solution.py:108
  407.4 1.8 convert_add_fusion.1
  409.3 1.7 copy-done.2
  411.6 0.8 fusion.55
  413.2 2.0 fusion.34
  415.3 1.0 broadcast_in_dim.93
  416.3 3.7 all-to-all-start.2
  420.0 12.2 %fusion.2 = bf16[1536,768]{0,1:T(8,128)(2,1)S(1)} fusion(bf16[1536,1344]{0,1:T(8,128)(2,1)} %reduce_sum.72, f32[768]{0:T(1024)S(1)} %copy-done.13), kind=kLoop, calls=%fused_computation.4 | loop fusion | flops 79036416 | bytes 4721664 | tf_op jit(solution)/shard_map/convert_element_type | solution.py:166
  432.2 4.2 fusion.57
  436.4 4.3 all-to-all-done.2
  440.7 3.1 add_convert_fusion
  443.8 1.6 copy.98
  445.5 7.4 %all-to-all-start.3 = ((bf16[16,2,48,768]{3,2,1,0:T(8,128)(2,1)}), bf16[16,2,48,768]{3,2,1,0:T(8,128)(2,1)S(1)}, u32[]{:S(2)}, u32[]{:S(2)}) async-start(bf16[16,2,48,768]{3,2,1,0:T(8,128)(2,1)} %bitcast.71), calls=%async_computation.3 | async-start | bytes 4718592 | tf_op jit(solution)/shard_map/all_to_all | solution.py:57
  452.9 1.6 constant_dynamic-slice_fusion.1
  454.5 1.6 copy.77
  456.2 26.4 %all-to-all-done.3 = bf16[16,2,48,768]{3,2,1,0:T(8,128)(2,1)S(1)} async-done(((bf16[16,2,48,768]{3,2,1,0:T(8,128)(2,1)}), bf16[16,2,48,768]{3,2,1,0:T(8,128)(2,1)S(1)}, u32[]{:S(2)}, u32[]{:S(2)}) %all-to-all-start.3) | async-done | bytes 2359328 | tf_op jit(solution)/shard_map/all_to_all | solution.py:57
  482.6 1.0 reduce_sum.74
  483.6 4.9 all-to-all-start.4
  488.5 1.1 constant_dynamic-slice_fusion
  490.3 6.7 %all-to-all-done.4 = bf16[2,48,768]{2,1,0:T(8,128)(2,1)S(1)} async-done(((bf16[2,48,768]{2,1,0:T(8,128)(2,1)}), bf16[2,48,768]{2,1,0:T(8,128)(2,1)S(1)}, u32[]{:S(2)}, u32[]{:S(2)}) %all-to-all-start.4) | async-done | bytes 147488 | tf_op jit(solution)/shard_map/all_to_all | solution.py:59
  497.0 1.5 fusion.41
  (80 shorter events, 7.8 us)
Async XLA Ops:
  7.2 61.8 %copy-start = (bf16[768,768]{1,0:T(8,128)(2,1)S(1)}, bf16[768,768]{1,0:T(8,128)(2,1)}, u32[]{:S(2)}) copy-start(bf16[768,768]{1,0:T(8,128)(2,1)} %param.24) | copy-start | bytes 3538948
  7.2 20.2 %collective-permute-start = (bf16[48,768]{1,0:T(8,128)(2,1)}, bf16[48,768]{1,0:T(8,128)(2,1)S(1)}, u32[]{:S(2)}, u32[]{:S(2)}) collective-permute-start(bf16[48,768]{1,0:T(8,128)(2,1)} %param.14), channel_id=1, source_target_pairs={{0,128},{128,0},{1,129},{129,1},{2,130},{130,2},{3,131},{131,3},{4... | collective-permute-start | bytes 221192 | tf_op jit(solution)/shard_map/ppermute | solution.py:83
  16.1 11.1 %all-to-all-start = ((f32[16,2,48]{2,1,0:T(2,128)}), f32[16,2,48]{2,1,0:T(2,128)S(1)}, u32[]{:S(2)}, u32[]{:S(2)}) async-start(f32[16,2,48]{2,1,0:T(2,128)} %broadcast_in_dim.49), calls=%async_computation | async-start | bytes 32768 | tf_op jit(solution)/shard_map/all_to_all | solution.py:87
  19.6 373.7 %all-gather.2.cloned.1.call-start = ((), (), s32[]{:S(2)}) async-start(), calls=%async_computation.5 | async-start | bytes 37158912 | tf_op jit(solution)/shard_map/all_gather | solution.py:108
  67.2 0.7 copy-start.6
  67.2 0.7 copy-start.7
  67.2 0.7 copy-start.8
  67.2 0.7 copy-start.9
  69.0 2.1 copy-start.15
  72.7 2.2 copy-start.5
  77.2 330.3 %copy-start.10 = (f32[576]{0:T(1024)S(1)}, f32[576]{0:T(1024)}, u32[]{:S(2)}) copy-start(f32[576]{0:T(1024)} %param.21) | copy-start | bytes 6916
  409.2 1.8 copy-start.2
  411.6 3.5 copy-start.3
  412.5 7.6 %copy-start.13 = (f32[768]{0:T(1024)S(1)}, f32[768]{0:T(1024)}, u32[]{:S(2)}) copy-start(f32[768]{0:T(1024)} %param.25) | copy-start | bytes 9220
  415.2 17.0 %copy-start.14 = (bf16[768,768]{1,0:T(8,128)(2,1)S(1)}, bf16[768,768]{1,0:T(8,128)(2,1)}, u32[]{:S(2)}) copy-start(bf16[768,768]{1,0:T(8,128)(2,1)} %param.26) | copy-start | bytes 3538948
  416.3 24.4 %all-to-all-start.2 = ((bf16[8,192,192]{2,1,0:T(8,128)(2,1)}), bf16[8,192,192]{2,1,0:T(8,128)(2,1)S(1)}, u32[]{:S(2)}, u32[]{:S(2)}) async-start(bf16[8,192,192]{2,1,0:T(8,128)(2,1)} %broadcast_in_dim.93), calls=%async_computation.2 | async-start | bytes 1572864 | tf_op jit(solution)/shard_map/all_to_all | solution.py:154
  432.2 8.5 %copy-start.4 = (bf16[192,768]{1,0:T(8,128)(2,1)S(1)}, bf16[192,768]{1,0:T(8,128)(2,1)}, u32[]{:S(2)}) copy-start(bf16[192,768]{1,0:T(8,128)(2,1)} %param.22) | copy-start | bytes 884740
  443.8 54.7 %copy-start.1 = (bf16[768,768]{1,0:T(8,128)(2,1)S(1)}, bf16[768,768]{1,0:T(8,128)(2,1)}, u32[]{:S(2)}) copy-start(bf16[768,768]{1,0:T(8,128)(2,1)} %param.24) | copy-start | bytes 3538948
  445.5 51.5 %copy-start.11 = (f32[768]{0:T(1024)S(1)}, f32[768]{0:T(1024)}, u32[]{:S(2)}) copy-start(f32[768]{0:T(1024)} %param.27) | copy-start | bytes 9220
  445.5 51.5 %copy-start.12 = (f32[768]{0:T(1024)S(1)}, f32[768]{0:T(1024)}, u32[]{:S(2)}) copy-start(f32[768]{0:T(1024)} %param.23) | copy-start | bytes 9220
  445.5 37.1 %all-to-all-start.3 = ((bf16[16,2,48,768]{3,2,1,0:T(8,128)(2,1)}), bf16[16,2,48,768]{3,2,1,0:T(8,128)(2,1)S(1)}, u32[]{:S(2)}, u32[]{:S(2)}) async-start(bf16[16,2,48,768]{3,2,1,0:T(8,128)(2,1)} %bitcast.71), calls=%async_computation.3 | async-start | bytes 4718592 | tf_op jit(solution)/shard_map/all_to_all | solution.py:57
  483.6 13.4 %all-to-all-start.4 = ((bf16[2,48,768]{2,1,0:T(8,128)(2,1)}), bf16[2,48,768]{2,1,0:T(8,128)(2,1)S(1)}, u32[]{:S(2)}, u32[]{:S(2)}) async-start(bf16[2,48,768]{2,1,0:T(8,128)(2,1)} %reduce_sum.74), calls=%async_computation.4 | async-start | bytes 294912 | tf_op jit(solution)/shard_map/all_to_all | solution.py:59
Sparse Core Ops, SparseCore 0:
  75.1 318.2 all-gather.1
